TPU v7x, 128 devices: a whole 4x4x4 slice. The times are simulated.
128 devices in a mesh: dp: 4 (over z_hi, core), mp: 32 (over x, y, z_lo).
Axes of the slice: x: 4, y: 4, z: 4 (z_hi: 2, z_lo: 2; z = z_hi * 2 + z_lo), core: 2. Of those that a mesh axis runs over, the one named last changes fastest.
Arguments:
- residual_input: bfloat16 [2048, 4608], P(('dp', 'mp')), may hold values from -6 to 6
- before_attention_gain: float32 [4608], replicated, may hold values from 0.25 to 1.75
- after_attention_gain: float32 [4608], replicated, may hold values from 0.25 to 1.75
- before_feedforward_gain: float32 [4608], replicated, may hold values from 0.25 to 1.75
- after_feedforward_gain: float32 [4608], replicated, may hold values from 0.25 to 1.75
- query_weight: bfloat16 [4608, 4096], P(None, 'mp'), may hold values from -0.09375 to 0.09375
- key_value_weight: bfloat16 [4608, 2, 32, 128], P(None, None, 'mp'), as said below
- output_weight: bfloat16 [4096, 4608], P('mp'), may hold values from -0.09375 to 0.09375
- gate_matrix: bfloat16 [4608, 20480], P(None, 'mp'), may hold values from -0.09375 to 0.09375
- up_matrix: bfloat16 [4608, 20480], P(None, 'mp'), may hold values from -0.09375 to 0.09375
- down_matrix: bfloat16 [20480, 4608], P('mp'), may hold values from -0.0390625 to 0.0390625
- key_value_cache: bfloat16 [256, 2, 32, 16, 128], P('dp', None, 'mp'), as said below
- projected_lowrank_left: bfloat16 [64, 4608, 16], P('mp'), may hold values from -0.09375 to 0.09375
- projected_lowrank_right: bfloat16 [64, 16, 3, 32, 128], P(None, None, None, 'mp'), as said below
- result_lowrank_left: bfloat16 [64, 4096, 16], P(None, 'mp'), may hold values from -0.09375 to 0.09375
- result_lowrank_right: bfloat16 [64, 16, 4608], P('mp'), may hold values from -1.5 to 1.5
- token_request: int32 [4, 512], P('dp'), may hold values from 0 to 7, never falling along the last dimension, each value on 1 to 256 neighbouring positions
- lowrank_choice_by_prompt: int32 [4, 8], P('dp'), may hold values from 0 to 63
- adapter_position: int32 [64], replicated, may hold values from 0 to 63, each once
- request_pages: int32 [4, 8, 4], replicated, may hold values from 0 to 255
Outputs:
- hidden_out: bfloat16 [2048, 4608], P(('dp', 'mp'))
- kv_new: bfloat16 [2048, 2, 32, 128], P('dp', None, 'mp')
Inputs may be any that keep to these rules, and one draw needn't show every extreme that they name: `key_value_weight`: query heads h and h2 with h // 2 == h2 // 2 have equal key and value weights: they share one key and value head. `key_value_cache`: query heads that share a key and value head have equal cached keys and values. `projected_lowrank_right`: the key and value parts of query heads that share a key and value head are equal. `token_request`: numbers never fall along a group; every request has at least one token. `adapter_position`: each slot once. `request_pages`: pages may repeat within and across requests.
All inputs are finite; a program needn't handle non-finite values.
Results may differ from a plain program's by a relative error of at most 0.035.
Values may be sent and summed in bfloat16 or wider, within the bound.
No kernel may reach another device: no remote copies, remote signals or barrier semaphores. Data moves between devices by JAX's collectives and lax.ppermute only.
A program may use at most 128 MiB of HBM per device.

v0:
```python
import math

import jax
import jax.numpy as jnp
from jax import lax
from jax.sharding import PartitionSpec as P

HIDDEN_BREADTH = 4608
ASKING_CHANNELS = 32
CHANNEL_LENGTH = 128
NUM_LOW_TERMS = 64
LOW_DIMENSION = 16
SHARD_PROMPTS = 8
PPR = 4
PAGE = 16


EPS = 1e-06
SOFTCAP = 50.0


def rms_scale(values, scaling):
    mean_square = jnp.mean(values * values, axis=-1, keepdims=True)
    return values * lax.rsqrt(mean_square + EPS) * scaling


def apply_rotary(values, token_positions):
    half_dim = values.shape[-1] // 2
    frequency = 10000.0 ** (-2.0 * jnp.arange(half_dim, dtype=jnp.float32) / values.shape[-1])
    angles = token_positions.astype(jnp.float32)[:, None] * frequency[None, :]
    cosine = jnp.cos(angles)[:, None, :]
    sine_part = jnp.sin(angles)[:, None, :]
    first_half = values[..., :half_dim]
    second_half = values[..., half_dim:]
    return jnp.concatenate(
        [
            first_half * cosine - second_half * sine_part,
            second_half * cosine + first_half * sine_part,
        ],
        axis=-1,
    )


def positions_of(segments):
    length = segments.shape[0]
    earlier = jnp.sum((segments[None, :] < segments[:, None]).astype(jnp.int32), axis=1)
    return PPR * PAGE + jnp.arange(length, dtype=jnp.int32) - earlier


def capped(scores):
    return SOFTCAP * jnp.tanh(scores / SOFTCAP)


def attend_local(query_rows, keys_new, fresh_values, keys_pre, values_pre, segments):
    scale_factor = 1.0 / math.sqrt(HIDDEN_BREADTH // ASKING_CHANNELS)
    length = segments.shape[0]
    prefix_owner = jnp.arange(keys_pre.shape[1], dtype=jnp.int32) // (PPR * PAGE)
    mask_pre = (prefix_owner[None, :] == segments[:, None])[None]
    ordinal = jnp.arange(length, dtype=jnp.int32)
    mask_new = ((segments[None, :] == segments[:, None]) & (ordinal[None, :] <= ordinal[:, None]))[
        None
    ]
    scores_pre = (
        jnp.einsum("thd,hjd->htj", query_rows, keys_pre, preferred_element_type=jnp.float32)
        * scale_factor
    )
    scores_new = (
        jnp.einsum("thd,uhd->htu", query_rows, keys_new, preferred_element_type=jnp.float32)
        * scale_factor
    )
    weight_pre = jnp.where(mask_pre, jnp.exp(capped(scores_pre)), 0.0)
    weight_new = jnp.where(mask_new, jnp.exp(capped(scores_new)), 0.0)
    totals = jnp.sum(weight_pre, axis=-1, keepdims=True) + jnp.sum(
        weight_new, axis=-1, keepdims=True
    )
    probs_pre = (weight_pre / totals).astype(jnp.bfloat16)
    probs_new = (weight_new / totals).astype(jnp.bfloat16)
    mixture = jnp.einsum("htj,hjd->thd", probs_pre, values_pre, preferred_element_type=jnp.float32)
    mixture = mixture + jnp.einsum(
        "htu,uhd->thd", probs_new, fresh_values, preferred_element_type=jnp.float32
    )
    return mixture.astype(jnp.bfloat16).reshape(length, -1)


def shards(
    residual_input,
    before_attention_gain,
    after_attention_gain,
    before_feedforward_gain,
    after_feedforward_gain,
    query_weight,
    key_value_weight,
    output_weight,
    gate_matrix,
    up_matrix,
    down_matrix,
    key_value_cache,
    projected_lowrank_left,
    projected_lowrank_right,
    result_lowrank_left,
    result_lowrank_right,
    token_request,
    lowrank_choice_by_prompt,
    adapter_position,
    request_pages,
):
    mp_index = lax.axis_index("mp")
    dp_index = lax.axis_index("dp")
    residual = residual_input.astype(jnp.float32)
    normed_rows = rms_scale(residual, before_attention_gain).astype(jnp.bfloat16)
    normalized_rows = lax.all_gather(normed_rows, "mp", axis=0, tiled=True)
    prompt_ordinal = normalized_rows.shape[0]
    channel_window = query_weight.shape[1] // CHANNEL_LENGTH
    query_rows = jnp.dot(normalized_rows, query_weight, preferred_element_type=jnp.float32).reshape(
        prompt_ordinal, channel_window, CHANNEL_LENGTH
    )
    key_value_rows = jnp.dot(
        normalized_rows,
        key_value_weight.reshape(HIDDEN_BREADTH, 2 * channel_window * CHANNEL_LENGTH),
        preferred_element_type=jnp.float32,
    ).reshape(prompt_ordinal, 2, channel_window, CHANNEL_LENGTH)
    segments = token_request[0]
    request_ids = lowrank_choice_by_prompt[0]
    request_range = jnp.arange(SHARD_PROMPTS, dtype=jnp.int32)
    membership = segments[:, None] == request_range[None, :]
    adapter_range = jnp.arange(NUM_LOW_TERMS, dtype=jnp.int32)
    token_adapter = jnp.sum(jnp.where(membership, request_ids[None, :], 0), axis=1)
    token_adapter_slot = jnp.sum(
        jnp.where(token_adapter[:, None] == adapter_range[None, :], adapter_position[None, :], 0),
        axis=1,
    )
    gathered_down = lax.all_gather(projected_lowrank_left, "mp", axis=0, tiled=True)
    request_slot = jnp.sum(
        jnp.where(request_ids[:, None] == adapter_range[None, :], adapter_position[None, :], 0),
        axis=1,
    )
    request_down = gathered_down[request_slot]
    request_factors = jnp.einsum(
        "td,rdk->trk", normalized_rows, request_down, preferred_element_type=jnp.float32
    )
    lowrank_source = jnp.sum(jnp.where(membership[:, :, None], request_factors, 0.0), axis=1)
    lowrank_source = lowrank_source.astype(jnp.bfloat16)
    choice_mask_table = membership.astype(jnp.bfloat16)
    broadened_lines = (choice_mask_table[:, :, None] * lowrank_source[:, None, :]).reshape(
        prompt_ordinal, SHARD_PROMPTS * LOW_DIMENSION
    )
    raised_result_lines = projected_lowrank_right[request_ids].reshape(
        SHARD_PROMPTS * LOW_DIMENSION, 3 * channel_window * CHANNEL_LENGTH
    )
    adapter_query_key_value = jnp.dot(
        broadened_lines, raised_result_lines, preferred_element_type=jnp.float32
    ).reshape(prompt_ordinal, 3, channel_window, CHANNEL_LENGTH)
    token_positions = positions_of(segments)
    rotary_queries = apply_rotary(
        query_rows + adapter_query_key_value[:, 0], token_positions
    ).astype(jnp.bfloat16)
    rotary_keys = apply_rotary(
        key_value_rows[:, 0] + adapter_query_key_value[:, 1], token_positions
    ).astype(jnp.bfloat16)
    fresh_values = (key_value_rows[:, 1] + adapter_query_key_value[:, 2]).astype(jnp.bfloat16)
    kv_new = jnp.stack([rotary_keys, fresh_values], axis=1)
    own_pages = lax.dynamic_index_in_dim(request_pages, dp_index, 0, keepdims=False).reshape(
        SHARD_PROMPTS * PPR
    )
    whole_pool = lax.all_gather(key_value_cache, "dp", axis=0, tiled=True)
    chosen = whole_pool[own_pages]
    keys_pre = jnp.transpose(chosen[:, 0], (1, 0, 2, 3)).reshape(
        channel_window, SHARD_PROMPTS * PPR * PAGE, CHANNEL_LENGTH
    )
    values_pre = jnp.transpose(chosen[:, 1], (1, 0, 2, 3)).reshape(
        channel_window, SHARD_PROMPTS * PPR * PAGE, CHANNEL_LENGTH
    )
    attended = attend_local(
        rotary_queries, rotary_keys, fresh_values, keys_pre, values_pre, segments
    )
    request_output_down = result_lowrank_left[request_ids]
    request_output_factors = jnp.einsum(
        "tc,rck->trk", attended, request_output_down, preferred_element_type=jnp.float32
    )
    output_adapter_piece = jnp.sum(
        jnp.where(membership[:, :, None], request_output_factors, 0.0), axis=1
    )
    result_lowrank_source = lax.psum(output_adapter_piece.astype(jnp.bfloat16), "mp")
    result_seat_lines = result_lowrank_right.shape[0]
    output_slots = mp_index * result_seat_lines + jnp.arange(result_seat_lines, dtype=jnp.int32)
    resident_here = (token_adapter_slot[:, None] == output_slots[None, :]).astype(jnp.bfloat16)
    broadened_result = (resident_here[:, :, None] * result_lowrank_source[:, None, :]).reshape(
        prompt_ordinal, result_seat_lines * LOW_DIMENSION
    )
    raised_window = result_lowrank_right.reshape(result_seat_lines * LOW_DIMENSION, HIDDEN_BREADTH)
    attn_sum = lax.psum_scatter(
        (
            jnp.dot(attended, output_weight, preferred_element_type=jnp.float32)
            + jnp.dot(broadened_result, raised_window, preferred_element_type=jnp.float32)
        ).astype(jnp.bfloat16),
        "mp",
        scatter_dimension=0,
        tiled=True,
    ).astype(jnp.float32)
    after_attn = (residual + rms_scale(attn_sum, after_attention_gain)).astype(jnp.bfloat16)
    normed_ffw = rms_scale(after_attn.astype(jnp.float32), before_feedforward_gain).astype(
        jnp.bfloat16
    )
    piece = lax.all_gather(normed_ffw, "mp", axis=0, tiled=True)
    gated = jnp.dot(piece, gate_matrix, preferred_element_type=jnp.float32)
    upward = jnp.dot(piece, up_matrix, preferred_element_type=jnp.float32)
    hidden = (jax.nn.gelu(gated, approximate=True) * upward).astype(jnp.bfloat16)
    ffw_sum = lax.psum_scatter(
        jnp.dot(hidden, down_matrix, preferred_element_type=jnp.float32).astype(jnp.bfloat16),
        "mp",
        scatter_dimension=0,
        tiled=True,
    ).astype(jnp.float32)
    hidden_out = (
        after_attn.astype(jnp.float32) + rms_scale(ffw_sum, after_feedforward_gain)
    ).astype(jnp.bfloat16)
    return (hidden_out, kv_new)


def solution(mesh):
    return jax.shard_map(
        shards,
        mesh=mesh,
        in_specs=(
            P(("dp", "mp"), None),
            P(),
            P(),
            P(),
            P(),
            P(None, "mp"),
            P(None, None, "mp", None),
            P("mp", None),
            P(None, "mp"),
            P(None, "mp"),
            P("mp", None),
            P("dp", None, "mp", None, None),
            P("mp", None, None),
            P(None, None, None, "mp", None),
            P(None, "mp", None),
            P("mp", None, None),
            P("dp", None),
            P("dp", None),
            P(),
            P(),
        ),
        out_specs=(P(("dp", "mp"), None), P("dp", None, "mp", None)),
        check_vma=False,
    )
```

profile of v0, /device:TPU:0, one launch (start us, length us, event | category | flops | bytes accessed | tf_op | source)
XLA Modules:
  0.0 1112.8 jit_solution(17951339612052338414)
XLA Ops:
  8.0 1.1 fusion.31
  9.0 1.7 fusion.33
  13.1 2.1 gather_fusion.3
  15.2 1.7 gather_fusion.2
  17.7 2.0 copy.60
  19.7 2.5 copy.50
  23.0 15.9 %all-gather.5.cloned.1.call-done = bf16[256,2,1,16,128]{4,3,2,1,0:T(8,128)(2,1)} async-done(((bf16[64,2,1,16,128]{4,3,2,1,0:T(8,128)(2,1)}), bf16[256,2,1,16,128]{4,3,2,1,0:T(8,128)(2,1)}) %all-gather.5.cloned.1.call-update) | async-done | bytes 2097168 | tf_op jit(solution)/shard_map/all_gather | solution.py:165
  38.9 2.2 gather_fusion
  41.2 157.9 %all-gather.7.cloned.1.call-done = bf16[512,4608]{1,0:T(8,128)(2,1)} async-done(((bf16[16,4608]{1,0:T(8,128)(2,1)}), bf16[512,4608]{1,0:T(8,128)(2,1)}) %all-gather.7.cloned.1.call-update) | async-done | bytes 4718608 | tf_op jit(solution)/shard_map/all_gather | solution.py:111
  199.1 4.5 fusion.19
  203.6 207.7 %all-gather.9.cloned.1.call-done = bf16[64,4608,16]{1,2,0:T(8,128)(2,1)} async-done(((bf16[2,4608,16]{1,2,0:T(8,128)(2,1)}), bf16[64,4608,16]{1,2,0:T(8,128)(2,1)}) %all-gather.9.cloned.1.call-update) | async-done | bytes 9437200 | tf_op jit(solution)/shard_map/all_gather | solution.py:132
  411.2 4.3 gather_fusion.1
  415.6 4.1 fusion.84
  420.1 1.7 fusion.22
  424.2 157.2 %psum.7 = bf16[512,16]{0,1:T(8,128)(2,1)S(1)} all-reduce(bf16[512,16]{0,1:T(8,128)(2,1)S(1)} %select_reduce_fusion), channel_id=1, replica_groups=mesh['dp'=4,'mp'=32] {'mp'}, use_global_device_ids=true, to_apply=%region_9.10 | all-reduce | flops 8192 | bytes 32768 | tf_op jit(solution)/shard_map/psum | solution.py:183
  581.4 1.4 fusion.63
  582.8 3.5 fusion
  586.4 165.2 %reduce-scatter.3.cloned.1.call-done = bf16[16,4608]{1,0:T(8,128)(2,1)} async-done(((bf16[512,4608]{1,0:T(8,128)(2,1)}), bf16[16,4608]{1,0:T(8,128)(2,1)}) %reduce-scatter.3.cloned.1.call-update) | async-done | bytes 147472 | tf_op jit(solution)/shard_map/reduce_scatter | solution.py:191
  752.7 1.2 fusion.35
  754.9 154.9 %all-gather.11.cloned.1.call-done = bf16[512,4608]{1,0:T(8,128)(2,1)} async-done(((bf16[16,4608]{1,0:T(8,128)(2,1)}), bf16[512,4608]{1,0:T(8,128)(2,1)}) %all-gather.11.cloned.1.call-update) | async-done | bytes 4718608 | tf_op jit(solution)/shard_map/all_gather | solution.py:204
  909.8 7.4 fusion.85
  917.2 14.2 %convolution_convert_fusion = bf16[512,4608]{1,0:T(8,128)(2,1)} fusion(bf16[640,4608]{1,0:T(8,128)(2,1)} %param.30, bf16[512,4608]{1,0:T(8,128)(2,1)} %all-gather.11.cloned.1.call-done, bf16[4608,640]{1,0:T(8,128)(2,1)} %param.29, f32[512,640]{1,0:T(8,128)S(1)} %fusion.85), kind=kOutput, calls=%fused_computation.6 | convolution fusion | flops 6045433856 | bytes 22544384 | tf_op jit(solution)/shard_map/dot_general | solution.py:209
  932.4 170.8 %reduce-scatter.5.cloned.1.call-done = bf16[16,4608]{1,0:T(8,128)(2,1)} async-done(((bf16[512,4608]{1,0:T(8,128)(2,1)}), bf16[16,4608]{1,0:T(8,128)(2,1)}) %reduce-scatter.5.cloned.1.call-update) | async-done | bytes 147472 | tf_op jit(solution)/shard_map/reduce_scatter | solution.py:208
  1104.3 1.7 fusion.38
  (87 shorter events, 11.4 us)
Async XLA Ops:
  7.2 575.7 %copy-start = (bf16[128,4608]{1,0:T(8,128)(2,1)S(1)}, bf16[128,4608]{1,0:T(8,128)(2,1)}, u32[]{:S(2)}) copy-start(bf16[128,4608]{1,0:T(8,128)(2,1)} %param.27) | copy-start | bytes 3538948
  7.2 31.8 %all-gather.5.cloned.1.call-start = ((), (), s32[]{:S(2)}) async-start(), calls=%async_computation.2 | async-start | bytes 2621440 | tf_op jit(solution)/shard_map/all_gather | solution.py:165
  7.9 191.1 %all-gather.7.cloned.1.call-start = ((), (), s32[]{:S(2)}) async-start(), calls=%async_computation.3 | async-start | bytes 4866048 | tf_op jit(solution)/shard_map/all_gather | solution.py:111
  10.7 400.5 %all-gather.9.cloned.1.call-start = ((), (), s32[]{:S(2)}) async-start(), calls=%async_computation.4 | async-start | bytes 9732096 | tf_op jit(solution)/shard_map/all_gather | solution.py:132
  11.5 740.1 %reduce-scatter.3.cloned.1.call-start = ((), (), s32[]{:S(2)}) async-start(), calls=%async_computation.5 | async-start | bytes 4866048 | tf_op jit(solution)/shard_map/reduce_scatter | solution.py:191
  17.7 4.6 copy-start.11
  17.7 4.6 copy-start.12
  17.7 4.8 copy-start.7
  415.5 4.2 copy-start.5
  415.5 4.6 slice-start
  415.6 4.6 copy-start.4
  415.6 4.6 slice-start.1
  422.9 1.0 copy-start.2
  423.4 158.0 %copy-start.6 = (bf16[2,16,4608]{2,1,0:T(8,128)(2,1)S(1)}, bf16[2,16,4608]{2,1,0:T(8,128)(2,1)}, u32[]{:S(2)}) copy-start(bf16[2,16,4608]{2,1,0:T(8,128)(2,1)} %param.35) | copy-start | bytes 884740
  586.4 166.3 %copy-start.3 = (bf16[16,4608]{1,0:T(8,128)(2,1)S(1)}, bf16[16,4608]{1,0:T(8,128)(2,1)}, u32[]{:S(2)}) copy-start(bf16[16,4608]{1,0:T(8,128)(2,1)} %param.20) | copy-start | bytes 442372
  586.4 166.3 %copy-start.8 = (f32[4608]{0:T(1024)S(1)}, f32[4608]{0:T(1024)}, u32[]{:S(2)}) copy-start(f32[4608]{0:T(1024)} %param.22) | copy-start | bytes 55300
  586.4 167.5 %copy-start.9 = (f32[4608]{0:T(1024)S(1)}, f32[4608]{0:T(1024)}, u32[]{:S(2)}) copy-start(f32[4608]{0:T(1024)} %param.23) | copy-start | bytes 55300
  586.4 323.4 %all-gather.11.cloned.1.call-start = ((), (), s32[]{:S(2)}) async-start(), calls=%async_computation.6 | async-start | bytes 4866048 | tf_op jit(solution)/shard_map/all_gather | solution.py:204
  754.7 348.5 %reduce-scatter.5.cloned.1.call-start = ((), (), s32[]{:S(2)}) async-start(), calls=%async_computation.7 | async-start | bytes 4866048 | tf_op jit(solution)/shard_map/reduce_scatter | solution.py:208
  917.2 188.7 %copy-start.1 = (bf16[128,4608]{1,0:T(8,128)(2,1)S(1)}, bf16[128,4608]{1,0:T(8,128)(2,1)}, u32[]{:S(2)}) copy-start(bf16[128,4608]{1,0:T(8,128)(2,1)} %param.27) | copy-start | bytes 3538948
  931.5 172.8 %copy-start.10 = (f32[4608]{0:T(1024)S(1)}, f32[4608]{0:T(1024)}, u32[]{:S(2)}) copy-start(f32[4608]{0:T(1024)} %param.24) | copy-start | bytes 55300
Sparse Core Ops, SparseCore 0:
  9.7 29.2 all-gather.4
  41.1 157.8 all-gather.6
  200.7 210.4 all-gather.8
  586.5 165.0 reduce-scatter.2
  754.8 154.9 all-gather.10
  931.6 171.5 reduce-scatter.4
where the time goes:
time: 1110 us
  waiting for transfers between devices  874 us (79%)
  blocking collectives  157 us (14%)
  matrix products  38.8 us (3%)
  local copies, waits for them, and re-layouts  17.5 us (2%)
  between operations  14.5 us (1%)
    all_gather x1, waiting for transfers between devices, shards(): lax.all_gather(projected_lowrank_left, 'mp', axis=0, tiled=True)  208 us
    reduce_scatter x1, waiting for transfers between devices, shards(): lax.psum_scatter(jnp.dot(hidden, down_matrix, preferred_element_type=jnp....  171 us
    reduce_scatter x1, waiting for transfers between devices, shards(): lax.psum_scatter((jnp.dot(attended, output_weight, preferred_element_type...  165 us
    all_gather x1, waiting for transfers between devices, shards(): normalized_rows = lax.all_gather(normed_rows, 'mp', axis=0, tiled=True)  158 us
    psum x1, blocking collectives, shards(): lax.psum(output_adapter_piece.astype(jnp.bfloat16), 'mp')  157 us
    all_gather x1, waiting for transfers between devices, shards(): piece = lax.all_gather(normed_ffw, 'mp', axis=0, tiled=True)  155 us
  transfers between devices with their start and end apart: 6, of which 6 were waited for; matrix products, arithmetic and copies ran while one was open for 2% of the time, Pallas kernels for 0%

commit v1 on v0

--- a/solution.py
+++ b/solution.py
@@ -17,6 +17,28 @@
 
 EPS = 1e-06
 SOFTCAP = 50.0
+
+DP_AXES = ("zh", "c")
+MP_AXES = ("x", "y", "zl")
+MP_STAGES = (("zl",), ("x", "y"))
+
+
+def gather_mp(values):
+    for stage in MP_STAGES:
+        values = lax.all_gather(values, stage, axis=0, tiled=True)
+    return values
+
+
+def scatter_mp(values):
+    for stage in reversed(MP_STAGES):
+        values = lax.psum_scatter(values, stage, scatter_dimension=0, tiled=True)
+    return values
+
+
+def sum_mp(values):
+    for stage in MP_STAGES:
+        values = lax.psum(values, stage)
+    return values
 
 
 def rms_scale(values, scaling):
@@ -104,11 +126,11 @@
     adapter_position,
     request_pages,
 ):
-    mp_index = lax.axis_index("mp")
-    dp_index = lax.axis_index("dp")
+    mp_index = lax.axis_index(MP_AXES)
+    dp_index = lax.axis_index(DP_AXES)
     residual = residual_input.astype(jnp.float32)
     normed_rows = rms_scale(residual, before_attention_gain).astype(jnp.bfloat16)
-    normalized_rows = lax.all_gather(normed_rows, "mp", axis=0, tiled=True)
+    normalized_rows = gather_mp(normed_rows)
     prompt_ordinal = normalized_rows.shape[0]
     channel_window = query_weight.shape[1] // CHANNEL_LENGTH
     query_rows = jnp.dot(normalized_rows, query_weight, preferred_element_type=jnp.float32).reshape(
@@ -129,17 +151,14 @@
         jnp.where(token_adapter[:, None] == adapter_range[None, :], adapter_position[None, :], 0),
         axis=1,
     )
-    gathered_down = lax.all_gather(projected_lowrank_left, "mp", axis=0, tiled=True)
-    request_slot = jnp.sum(
-        jnp.where(request_ids[:, None] == adapter_range[None, :], adapter_position[None, :], 0),
-        axis=1,
-    )
-    request_down = gathered_down[request_slot]
-    request_factors = jnp.einsum(
-        "td,rdk->trk", normalized_rows, request_down, preferred_element_type=jnp.float32
-    )
-    lowrank_source = jnp.sum(jnp.where(membership[:, :, None], request_factors, 0.0), axis=1)
-    lowrank_source = lowrank_source.astype(jnp.bfloat16)
+    seat_count = projected_lowrank_left.shape[0]
+    local_seats = mp_index * seat_count + jnp.arange(seat_count, dtype=jnp.int32)
+    seat_factors = jnp.einsum(
+        "td,sdk->tsk", normalized_rows, projected_lowrank_left, preferred_element_type=jnp.float32
+    )
+    seat_here = token_adapter_slot[:, None] == local_seats[None, :]
+    lowrank_source = jnp.sum(jnp.where(seat_here[:, :, None], seat_factors, 0.0), axis=1)
+    lowrank_source = sum_mp(lowrank_source.astype(jnp.bfloat16))
     choice_mask_table = membership.astype(jnp.bfloat16)
     broadened_lines = (choice_mask_table[:, :, None] * lowrank_source[:, None, :]).reshape(
         prompt_ordinal, SHARD_PROMPTS * LOW_DIMENSION
@@ -162,7 +181,7 @@
     own_pages = lax.dynamic_index_in_dim(request_pages, dp_index, 0, keepdims=False).reshape(
         SHARD_PROMPTS * PPR
     )
-    whole_pool = lax.all_gather(key_value_cache, "dp", axis=0, tiled=True)
+    whole_pool = lax.all_gather(key_value_cache, DP_AXES, axis=0, tiled=True)
     chosen = whole_pool[own_pages]
     keys_pre = jnp.transpose(chosen[:, 0], (1, 0, 2, 3)).reshape(
         channel_window, SHARD_PROMPTS * PPR * PAGE, CHANNEL_LENGTH
@@ -180,7 +199,7 @@
     output_adapter_piece = jnp.sum(
         jnp.where(membership[:, :, None], request_output_factors, 0.0), axis=1
     )
-    result_lowrank_source = lax.psum(output_adapter_piece.astype(jnp.bfloat16), "mp")
+    result_lowrank_source = sum_mp(output_adapter_piece).astype(jnp.bfloat16)
     result_seat_lines = result_lowrank_right.shape[0]
     output_slots = mp_index * result_seat_lines + jnp.arange(result_seat_lines, dtype=jnp.int32)
     resident_here = (token_adapter_slot[:, None] == output_slots[None, :]).astype(jnp.bfloat16)
@@ -188,28 +207,22 @@
         prompt_ordinal, result_seat_lines * LOW_DIMENSION
     )
     raised_window = result_lowrank_right.reshape(result_seat_lines * LOW_DIMENSION, HIDDEN_BREADTH)
-    attn_sum = lax.psum_scatter(
+    attn_sum = scatter_mp(
         (
             jnp.dot(attended, output_weight, preferred_element_type=jnp.float32)
             + jnp.dot(broadened_result, raised_window, preferred_element_type=jnp.float32)
-        ).astype(jnp.bfloat16),
-        "mp",
-        scatter_dimension=0,
-        tiled=True,
+        ).astype(jnp.bfloat16)
     ).astype(jnp.float32)
     after_attn = (residual + rms_scale(attn_sum, after_attention_gain)).astype(jnp.bfloat16)
     normed_ffw = rms_scale(after_attn.astype(jnp.float32), before_feedforward_gain).astype(
         jnp.bfloat16
     )
-    piece = lax.all_gather(normed_ffw, "mp", axis=0, tiled=True)
+    piece = gather_mp(normed_ffw)
     gated = jnp.dot(piece, gate_matrix, preferred_element_type=jnp.float32)
     upward = jnp.dot(piece, up_matrix, preferred_element_type=jnp.float32)
     hidden = (jax.nn.gelu(gated, approximate=True) * upward).astype(jnp.bfloat16)
-    ffw_sum = lax.psum_scatter(
-        jnp.dot(hidden, down_matrix, preferred_element_type=jnp.float32).astype(jnp.bfloat16),
-        "mp",
-        scatter_dimension=0,
-        tiled=True,
+    ffw_sum = scatter_mp(
+        jnp.dot(hidden, down_matrix, preferred_element_type=jnp.float32).astype(jnp.bfloat16)
     ).astype(jnp.float32)
     hidden_out = (
         after_attn.astype(jnp.float32) + rms_scale(ffw_sum, after_feedforward_gain)
@@ -218,31 +231,34 @@
 
 
 def solution(mesh):
+    fine_mesh = jax.sharding.Mesh(
+        mesh.devices.reshape(2, 2, 4, 4, 2), DP_AXES + MP_AXES
+    )
     return jax.shard_map(
         shards,
-        mesh=mesh,
+        mesh=fine_mesh,
         in_specs=(
-            P(("dp", "mp"), None),
-            P(),
-            P(),
-            P(),
-            P(),
-            P(None, "mp"),
-            P(None, None, "mp", None),
-            P("mp", None),
-            P(None, "mp"),
-            P(None, "mp"),
-            P("mp", None),
-            P("dp", None, "mp", None, None),
-            P("mp", None, None),
-            P(None, None, None, "mp", None),
-            P(None, "mp", None),
-            P("mp", None, None),
-            P("dp", None),
-            P("dp", None),
+            P(DP_AXES + MP_AXES, None),
+            P(),
+            P(),
+            P(),
+            P(),
+            P(None, MP_AXES),
+            P(None, None, MP_AXES, None),
+            P(MP_AXES, None),
+            P(None, MP_AXES),
+            P(None, MP_AXES),
+            P(MP_AXES, None),
+            P(DP_AXES, None, MP_AXES, None, None),
+            P(MP_AXES, None, None),
+            P(None, None, None, MP_AXES, None),
+            P(None, MP_AXES, None),
+            P(MP_AXES, None, None),
+            P(DP_AXES, None),
+            P(DP_AXES, None),
             P(),
             P(),
         ),
-        out_specs=(P(("dp", "mp"), None), P("dp", None, "mp", None)),
+        out_specs=(P(DP_AXES + MP_AXES, None), P(DP_AXES, None, MP_AXES, None)),
         check_vma=False,
     )

time: 1110 us -> 554 us (0.50)
  waiting for transfers between devices: 874 us -> 300 us
  blocking collectives: 157 us -> 171 us
    all_gather x4 -> x3, waiting for transfers between devices: 536 us -> 113 us  [the longest x2 105 us: gather_mp(): values = lax.all_gather(values, stage, axis=0, tiled=True)]
    reduce_scatter x2 -> x4, waiting for transfers between devices: 336 us -> 186 us  [scatter_mp(): values = lax.psum_scatter(values, stage, scatter_dimension=0, tiled=True)]
    all_gather x0 -> x2, blocking collectives: none -> 12.8 us  [gather_mp(): values = lax.all_gather(values, stage, axis=0, tiled=True)]
    psum x1 -> x4, blocking collectives: 157 us -> 158 us  [sum_mp(): values = lax.psum(values, stage)]
  transfers between devices with their start and end apart: 6 -> 7, of which waited for: 6 -> 7; matrix products, arithmetic and copies ran while one was open for 2% -> 4% of each run, Pallas kernels for 0% -> 0%
where the time goes in v1:
time: 554 us; the launch traced here: 553 us
  waiting for transfers between devices  300 us (54%)
  blocking collectives  171 us (31%)
  matrix products  39 us (7%)
  local copies, waits for them, and re-layouts  15.6 us (3%)
  between operations  14.6 us (3%)
  other arithmetic  12.7 us (2%)
    reduce_scatter x4, waiting for transfers between devices, scatter_mp(): values = lax.psum_scatter(values, stage, scatter_dimension=0, tiled=True)  186 us
    psum x4, blocking collectives, sum_mp(): values = lax.psum(values, stage)  158 us
    all_gather x2, waiting for transfers between devices, gather_mp(): values = lax.all_gather(values, stage, axis=0, tiled=True)  105 us
    dot_general x1, matrix products, shards(): jnp.dot(hidden, down_matrix, preferred_element_type=jnp.float32)  14.3 us
    all_gather x2, blocking collectives, gather_mp(): values = lax.all_gather(values, stage, axis=0, tiled=True)  12.8 us
  transfers between devices with their start and end apart: 7, of which 7 were waited for; matrix products, arithmetic and copies ran while one was open for 4% of the time, Pallas kernels for 0%

profile of v1, /device:TPU:0, one launch (start us, length us, event | category | flops | bytes accessed | tf_op | source)
XLA Modules:
  0.0 553.1 jit_solution(13675936725571163932)
XLA Ops:
  10.1 6.6 %all_gather.16 = bf16[32,4608]{1,0:T(8,128)(2,1)} all-gather(bf16[16,4608]{1,0:T(8,128)(2,1)S(1)} %fusion.33), channel_id=1, replica_groups=mesh['zh'=2,'c'=2,'x'=4,'y'=4,'zl'=2] {'zl'}, dimensions={0}, use_global_device_ids=true | all-gather | bytes 442368 | tf_op jit(solution)/shard_map/all_gather | solution.py:28
  18.3 2.1 gather_fusion.2
  20.4 1.7 gather_fusion.1
  23.0 2.0 copy.60
  25.0 2.5 copy.50
  31.0 8.0 %all-gather.4.cloned.1.call-done = bf16[256,2,1,16,128]{4,3,2,1,0:T(8,128)(2,1)} async-done(((bf16[64,2,1,16,128]{4,3,2,1,0:T(8,128)(2,1)}), bf16[256,2,1,16,128]{4,3,2,1,0:T(8,128)(2,1)}) %all-gather.4.cloned.1.call-update) | async-done | bytes 2097168 | tf_op jit(solution)/shard_map/all_gather | solution.py:184
  38.9 2.9 gather_fusion
  43.5 50.5 %all-gather.6.cloned.1.call-done = bf16[512,4608]{1,0:T(8,128)(2,1)} async-done(((bf16[32,4608]{1,0:T(8,128)(2,1)}), bf16[512,4608]{1,0:T(8,128)(2,1)}) %all-gather.6.cloned.1.call-update) | async-done | bytes 4718608 | tf_op jit(solution)/shard_map/all_gather | solution.py:28
  94.0 3.8 fusion.84
  97.9 8.8 %psum.28 = bf16[512,16]{0,1:T(8,128)(2,1)} all-reduce(bf16[512,16]{0,1:T(8,128)(2,1)S(1)} %select_reduce_fusion.2), channel_id=1, replica_groups=mesh['zh'=2,'c'=2,'x'=4,'y'=4,'zl'=2] {'zl'}, use_global_device_ids=true, to_apply=%region_4.5 | all-reduce | flops 8192 | bytes 32768 | tf_op jit(solution)/shard_map/psum | solution.py:40
  106.7 72.4 %psum.29 = bf16[512,16]{0,1:T(8,128)(2,1)S(1)} all-reduce(bf16[512,16]{0,1:T(8,128)(2,1)} %psum.28), channel_id=1, replica_groups=mesh['zh'=2,'c'=2,'x'=4,'y'=4,'zl'=2] {'x','y'}, use_global_device_ids=true, to_apply=%region_5.6 | all-reduce | flops 8192 | bytes 32768 | tf_op jit(solution)/shard_map/psum | solution.py:40
  181.1 3.9 fusion.19
  189.3 7.3 %psum.30 = f32[512,16]{0,1:T(8,128)S(1)} all-reduce(f32[512,16]{0,1:T(8,128)S(1)} %select_reduce_fusion), channel_id=1, replica_groups=mesh['zh'=2,'c'=2,'x'=4,'y'=4,'zl'=2] {'zl'}, use_global_device_ids=true, to_apply=%region_10.11 | all-reduce | flops 8192 | bytes 65536 | tf_op jit(solution)/shard_map/psum | solution.py:40
  196.6 69.5 %psum.31 = bf16[512,16]{0,1:T(8,128)(2,1)S(1)} all-reduce(f32[512,16]{0,1:T(8,128)S(1)} %psum.30), channel_id=1, replica_groups=mesh['zh'=2,'c'=2,'x'=4,'y'=4,'zl'=2] {'x','y'}, use_global_device_ids=true, to_apply=%region_11.12 | all-reduce | flops 8192 | bytes 49152 | tf_op jit(solution)/shard_map/psum | solution.py:40
  267.6 3.5 fusion
  271.2 75.6 %reduce-scatter.5.cloned.1.call-done = bf16[32,4608]{1,0:T(8,128)(2,1)} async-done(((bf16[512,4608]{1,0:T(8,128)(2,1)}), bf16[32,4608]{1,0:T(8,128)(2,1)}) %reduce-scatter.5.cloned.1.call-update) | async-done | bytes 294928 | tf_op jit(solution)/shard_map/reduce_scatter | solution.py:34
  346.9 16.2 %reduce-scatter.7.cloned.1.call-done = bf16[16,4608]{1,0:T(8,128)(2,1)} async-done(((bf16[32,4608]{1,0:T(8,128)(2,1)}), bf16[16,4608]{1,0:T(8,128)(2,1)}) %reduce-scatter.7.cloned.1.call-update) | async-done | bytes 147472 | tf_op jit(solution)/shard_map/reduce_scatter | solution.py:34
  365.4 6.2 %all_gather.18 = bf16[32,4608]{1,0:T(8,128)(2,1)} all-gather(bf16[16,4608]{1,0:T(8,128)(2,1)S(1)} %fusion.37), channel_id=1, replica_groups=mesh['zh'=2,'c'=2,'x'=4,'y'=4,'zl'=2] {'zl'}, dimensions={0}, use_global_device_ids=true | all-gather | bytes 442368 | tf_op jit(solution)/shard_map/all_gather | solution.py:28
  371.9 54.6 %all-gather.8.cloned.1.call-done = bf16[512,4608]{1,0:T(8,128)(2,1)} async-done(((bf16[32,4608]{1,0:T(8,128)(2,1)}), bf16[512,4608]{1,0:T(8,128)(2,1)}) %all-gather.8.cloned.1.call-update) | async-done | bytes 4718608 | tf_op jit(solution)/shard_map/all_gather | solution.py:28
  426.4 7.4 %fusion.85 = f32[512,640]{1,0:T(8,128)S(1)} fusion(bf16[512,4608]{1,0:T(8,128)(2,1)} %all-gather.8.cloned.1.call-done, bf16[4608,640]{1,0:T(8,128)(2,1)} %param.28), kind=kOutput, calls=%fused_computation.141 | convolution fusion | flops 3019898880 | bytes 11927552 | tf_op jit(solution)/shard_map/dot_general | solution.py:221
  433.9 14.3 %convolution_convert_fusion = bf16[512,4608]{1,0:T(8,128)(2,1)} fusion(bf16[640,4608]{1,0:T(8,128)(2,1)} %param.30, bf16[512,4608]{1,0:T(8,128)(2,1)} %all-gather.8.cloned.1.call-done, bf16[4608,640]{1,0:T(8,128)(2,1)} %param.29, f32[512,640]{1,0:T(8,128)S(1)} %fusion.85), kind=kOutput, calls=%fused_computation.5 | convolution fusion | flops 6045433856 | bytes 22544384 | tf_op jit(solution)/shard_map/dot_general | solution.py:225
  448.2 78.9 %reduce-scatter.9.cloned.1.call-done = bf16[32,4608]{1,0:T(8,128)(2,1)} async-done(((bf16[512,4608]{1,0:T(8,128)(2,1)}), bf16[32,4608]{1,0:T(8,128)(2,1)}) %reduce-scatter.9.cloned.1.call-update) | async-done | bytes 294928 | tf_op jit(solution)/shard_map/reduce_scatter | solution.py:34
  528.0 15.4 %reduce-scatter.11.cloned.1.call-done = bf16[16,4608]{1,0:T(8,128)(2,1)} async-done(((bf16[32,4608]{1,0:T(8,128)(2,1)}), bf16[16,4608]{1,0:T(8,128)(2,1)}) %reduce-scatter.11.cloned.1.call-update) | async-done | bytes 147472 | tf_op jit(solution)/shard_map/reduce_scatter | solution.py:34
  544.5 1.7 fusion.38
  (109 shorter events, 22.6 us)
Async XLA Ops:
  7.2 260.4 %copy-start = (bf16[128,4608]{1,0:T(8,128)(2,1)S(1)}, bf16[128,4608]{1,0:T(8,128)(2,1)}, u32[]{:S(2)}) copy-start(bf16[128,4608]{1,0:T(8,128)(2,1)} %param.27) | copy-start | bytes 3538948
  7.2 31.8 %all-gather.4.cloned.1.call-start = ((), (), s32[]{:S(2)}) async-start(), calls=%async_computation.4 | async-start | bytes 2621440 | tf_op jit(solution)/shard_map/all_gather | solution.py:184
  7.9 86.1 %all-gather.6.cloned.1.call-start = ((), (), s32[]{:S(2)}) async-start(), calls=%async_computation.5 | async-start | bytes 5013504 | tf_op jit(solution)/shard_map/all_gather | solution.py:28
  16.7 330.1 %reduce-scatter.5.cloned.1.call-start = ((), (), s32[]{:S(2)}) async-start(), calls=%async_computation.6 | async-start | bytes 5013504 | tf_op jit(solution)/shard_map/reduce_scatter | solution.py:34
  23.0 5.7 %copy-start.9 = (s32[1,512]{1,0:T(1,128)S(1)}, s32[1,512]{1,0:T(1,128)}, u32[]{:S(2)}) copy-start(s32[1,512]{1,0:T(1,128)} %param.36) | copy-start | bytes 6148
  23.0 5.8 %copy-start.19 = (s32[1,8]{1,0:T(1,128)S(1)}, s32[1,8]{1,0:T(1,128)}, u32[]{:S(2)}) copy-start(s32[1,8]{1,0:T(1,128)} %param.37) | copy-start | bytes 100
  23.0 5.8 %copy-start.20 = (s32[64]{0:T(128)S(1)}, s32[64]{0:T(128)}, u32[]{:S(2)}) copy-start(s32[64]{0:T(128)} %param.38) | copy-start | bytes 772
  27.5 153.6 %copy-start.3 = (bf16[256,4608]{1,0:T(8,128)(2,1)S(1)}, bf16[256,4608]{1,0:T(8,128)(2,1)}, u32[]{:S(2)}) copy-start(bf16[256,4608]{1,0:T(8,128)(2,1)} %copy.50) | copy-start | bytes 7077892
  94.0 3.8 copy-start.17
  179.8 5.3 slice-start
  181.1 4.0 slice-start.1
  181.1 4.0 copy-start.5
  185.2 2.4 copy-start.8
  188.5 77.7 %copy-start.6 = (bf16[2,16,4608]{2,1,0:T(8,128)(2,1)S(1)}, bf16[2,16,4608]{2,1,0:T(8,128)(2,1)}, u32[]{:S(2)}) copy-start(bf16[2,16,4608]{2,1,0:T(8,128)(2,1)} %param.35) | copy-start | bytes 884740
  188.5 77.6 %copy-start.15 = (bf16[512,2]{0,1:T(2,128)(2,1)S(1)}, bf16[512,2]{0,1:T(2,128)(2,1)}, u32[]{:S(2)}) copy-start(bf16[512,2]{0,1:T(2,128)(2,1)} %get-tuple-element.14) | copy-start | bytes 6148
  271.1 93.0 %copy-start.4 = (bf16[16,4608]{1,0:T(8,128)(2,1)S(1)}, bf16[16,4608]{1,0:T(8,128)(2,1)}, u32[]{:S(2)}) copy-start(bf16[16,4608]{1,0:T(8,128)(2,1)} %param.20) | copy-start | bytes 442372
  271.1 93.0 %copy-start.11 = (f32[4608]{0:T(1024)S(1)}, f32[4608]{0:T(1024)}, u32[]{:S(2)}) copy-start(f32[4608]{0:T(1024)} %param.22) | copy-start | bytes 55300
  271.1 94.1 %copy-start.12 = (f32[4608]{0:T(1024)S(1)}, f32[4608]{0:T(1024)}, u32[]{:S(2)}) copy-start(f32[4608]{0:T(1024)} %param.23) | copy-start | bytes 55300
  271.2 91.9 %reduce-scatter.7.cloned.1.call-start = ((), (), s32[]{:S(2)}) async-start(), calls=%async_computation.7 | async-start | bytes 442368 | tf_op jit(solution)/shard_map/reduce_scatter | solution.py:34
  346.8 79.6 %all-gather.8.cloned.1.call-start = ((), (), s32[]{:S(2)}) async-start(), calls=%async_computation.8 | async-start | bytes 5013504 | tf_op jit(solution)/shard_map/all_gather | solution.py:28
  371.6 155.5 %reduce-scatter.9.cloned.1.call-start = ((), (), s32[]{:S(2)}) async-start(), calls=%async_computation.9 | async-start | bytes 5013504 | tf_op jit(solution)/shard_map/reduce_scatter | solution.py:34
  433.8 112.4 %copy-start.1 = (bf16[128,4608]{1,0:T(8,128)(2,1)S(1)}, bf16[128,4608]{1,0:T(8,128)(2,1)}, u32[]{:S(2)}) copy-start(bf16[128,4608]{1,0:T(8,128)(2,1)} %param.27) | copy-start | bytes 3538948
  448.2 96.3 %copy-start.13 = (f32[4608]{0:T(1024)S(1)}, f32[4608]{0:T(1024)}, u32[]{:S(2)}) copy-start(f32[4608]{0:T(1024)} %param.24) | copy-start | bytes 55300
  448.2 95.3 %reduce-scatter.11.cloned.1.call-start = ((), (), s32[]{:S(2)}) async-start(), calls=%async_computation.10 | async-start | bytes 442368 | tf_op jit(solution)/shard_map/reduce_scatter | solution.py:34
  (7 other events, 12.2 us)
Sparse Core Ops, SparseCore 0:
  9.7 29.2 all-gather.3
  41.1 52.8 all-gather.5
  271.3 75.4 reduce-scatter.4
  349.0 13.9 reduce-scatter.6
  371.7 54.6 all-gather.7
  448.3 78.7 reduce-scatter.8
  529.4 13.9 reduce-scatter.10

commit v2 on v1

--- a/solution.py
+++ b/solution.py
@@ -36,7 +36,7 @@
 
 
 def sum_mp(values):
-    for stage in MP_STAGES:
+    for stage in (("zl",), ("y",), ("x",)):
         values = lax.psum(values, stage)
     return values
 
@@ -158,7 +158,7 @@
     )
     seat_here = token_adapter_slot[:, None] == local_seats[None, :]
     lowrank_source = jnp.sum(jnp.where(seat_here[:, :, None], seat_factors, 0.0), axis=1)
-    lowrank_source = sum_mp(lowrank_source.astype(jnp.bfloat16))
+    lowrank_source = sum_mp(lowrank_source).astype(jnp.bfloat16)
     choice_mask_table = membership.astype(jnp.bfloat16)
     broadened_lines = (choice_mask_table[:, :, None] * lowrank_source[:, None, :]).reshape(
         prompt_ordinal, SHARD_PROMPTS * LOW_DIMENSION

time: 554 us -> 480 us (0.87)
  blocking collectives: 171 us -> 93.7 us
    psum x4 -> x6, blocking collectives: 158 us -> 80.9 us  [sum_mp(): values = lax.psum(values, stage)]
  transfers between devices with their start and end apart: 7 -> 7, of which waited for: 7 -> 7; matrix products, arithmetic and copies ran while one was open for 4% -> 5% of each run, Pallas kernels for 0% -> 0%
where the time goes in v2:
time: 480 us; the launch traced here: 479 us
  waiting for transfers between devices  302 us (63%)
  blocking collectives  93.7 us (20%)
  matrix products  39 us (8%)
  local copies, waits for them, and re-layouts  15.6 us (3%)
  between operations  14.6 us (3%)
  other arithmetic  13.3 us (3%)
    reduce_scatter x4, waiting for transfers between devices, scatter_mp(): values = lax.psum_scatter(values, stage, scatter_dimension=0, tiled=True)  188 us
    all_gather x2, waiting for transfers between devices, gather_mp(): values = lax.all_gather(values, stage, axis=0, tiled=True)  105 us
    psum x6, blocking collectives, sum_mp(): values = lax.psum(values, stage)  80.9 us
    dot_general x1, matrix products, shards(): jnp.dot(hidden, down_matrix, preferred_element_type=jnp.float32)  14.3 us
    all_gather x2, blocking collectives, gather_mp(): values = lax.all_gather(values, stage, axis=0, tiled=True)  12.8 us
  transfers between devices with their start and end apart: 7, of which 7 were waited for; matrix products, arithmetic and copies ran while one was open for 5% of the time, Pallas kernels for 0%

profile of v2, /device:TPU:0, one launch (start us, length us, event | category | flops | bytes accessed | tf_op | source)
XLA Modules:
  0.0 478.9 jit_solution(8887985877023786385)
XLA Ops:
  10.1 6.6 %all_gather.16 = bf16[32,4608]{1,0:T(8,128)(2,1)} all-gather(bf16[16,4608]{1,0:T(8,128)(2,1)S(1)} %fusion.33), channel_id=1, replica_groups=mesh['zh'=2,'c'=2,'x'=4,'y'=4,'zl'=2] {'zl'}, dimensions={0}, use_global_device_ids=true | all-gather | bytes 442368 | tf_op jit(solution)/shard_map/all_gather | solution.py:28
  18.3 2.1 gather_fusion.2
  23.0 2.0 copy.60
  25.0 2.5 copy.50
  30.9 8.0 %all-gather.4.cloned.1.call-done = bf16[256,2,1,16,128]{4,3,2,1,0:T(8,128)(2,1)} async-done(((bf16[64,2,1,16,128]{4,3,2,1,0:T(8,128)(2,1)}), bf16[256,2,1,16,128]{4,3,2,1,0:T(8,128)(2,1)}) %all-gather.4.cloned.1.call-update) | async-done | bytes 2097168 | tf_op jit(solution)/shard_map/all_gather | solution.py:184
  38.9 2.9 gather_fusion
  43.5 50.5 %all-gather.6.cloned.1.call-done = bf16[512,4608]{1,0:T(8,128)(2,1)} async-done(((bf16[32,4608]{1,0:T(8,128)(2,1)}), bf16[512,4608]{1,0:T(8,128)(2,1)}) %all-gather.6.cloned.1.call-update) | async-done | bytes 4718608 | tf_op jit(solution)/shard_map/all_gather | solution.py:28
  94.0 3.8 fusion.84
  98.5 9.8 %psum.42 = f32[512,16]{0,1:T(8,128)} all-reduce(f32[512,16]{0,1:T(8,128)} %select_reduce_fusion.2), channel_id=1, replica_groups=mesh['zh'=2,'c'=2,'x'=4,'y'=4,'zl'=2] {'zl'}, use_global_device_ids=true, to_apply=%region_4.5 | all-reduce | flops 8192 | bytes 65536 | tf_op jit(solution)/shard_map/psum | solution.py:40
  108.3 18.2 %psum.43 = f32[512,16]{0,1:T(8,128)} all-reduce(f32[512,16]{0,1:T(8,128)} %psum.42), channel_id=1, replica_groups=mesh['zh'=2,'c'=2,'x'=4,'y'=4,'zl'=2] {'y'}, use_global_device_ids=true, to_apply=%region_5.6 | all-reduce | flops 8192 | bytes 65536 | tf_op jit(solution)/shard_map/psum | solution.py:40
  126.5 15.8 %psum.44 = bf16[512,16]{0,1:T(8,128)(2,1)S(1)} all-reduce(f32[512,16]{0,1:T(8,128)} %psum.43), channel_id=1, replica_groups=mesh['zh'=2,'c'=2,'x'=4,'y'=4,'zl'=2] {'x'}, use_global_device_ids=true, to_apply=%region_6.7 | all-reduce | flops 8192 | bytes 49152 | tf_op jit(solution)/shard_map/psum | solution.py:40
  144.3 3.9 fusion.19
  152.5 7.2 %psum.45 = f32[512,16]{0,1:T(8,128)S(1)} all-reduce(f32[512,16]{0,1:T(8,128)S(1)} %select_reduce_fusion), channel_id=1, replica_groups=mesh['zh'=2,'c'=2,'x'=4,'y'=4,'zl'=2] {'zl'}, use_global_device_ids=true, to_apply=%region_11.12 | all-reduce | flops 8192 | bytes 65536 | tf_op jit(solution)/shard_map/psum | solution.py:40
  159.7 15.5 %psum.46 = f32[512,16]{0,1:T(8,128)S(1)} all-reduce(f32[512,16]{0,1:T(8,128)S(1)} %psum.45), channel_id=1, replica_groups=mesh['zh'=2,'c'=2,'x'=4,'y'=4,'zl'=2] {'y'}, use_global_device_ids=true, to_apply=%region_12.13 | all-reduce | flops 8192 | bytes 65536 | tf_op jit(solution)/shard_map/psum | solution.py:40
  175.2 14.4 %psum.47 = bf16[512,16]{0,1:T(8,128)(2,1)S(1)} all-reduce(f32[512,16]{0,1:T(8,128)S(1)} %psum.46), channel_id=1, replica_groups=mesh['zh'=2,'c'=2,'x'=4,'y'=4,'zl'=2] {'x'}, use_global_device_ids=true, to_apply=%region_13.14 | all-reduce | flops 8192 | bytes 49152 | tf_op jit(solution)/shard_map/psum | solution.py:40
  191.0 3.5 fusion
  194.7 77.9 %reduce-scatter.5.cloned.1.call-done = bf16[32,4608]{1,0:T(8,128)(2,1)} async-done(((bf16[512,4608]{1,0:T(8,128)(2,1)}), bf16[32,4608]{1,0:T(8,128)(2,1)}) %reduce-scatter.5.cloned.1.call-update) | async-done | bytes 294928 | tf_op jit(solution)/shard_map/reduce_scatter | solution.py:34
  272.7 16.1 %reduce-scatter.7.cloned.1.call-done = bf16[16,4608]{1,0:T(8,128)(2,1)} async-done(((bf16[32,4608]{1,0:T(8,128)(2,1)}), bf16[16,4608]{1,0:T(8,128)(2,1)}) %reduce-scatter.7.cloned.1.call-update) | async-done | bytes 147472 | tf_op jit(solution)/shard_map/reduce_scatter | solution.py:34
  291.2 6.2 %all_gather.18 = bf16[32,4608]{1,0:T(8,128)(2,1)} all-gather(bf16[16,4608]{1,0:T(8,128)(2,1)S(1)} %fusion.37), channel_id=1, replica_groups=mesh['zh'=2,'c'=2,'x'=4,'y'=4,'zl'=2] {'zl'}, dimensions={0}, use_global_device_ids=true | all-gather | bytes 442368 | tf_op jit(solution)/shard_map/all_gather | solution.py:28
  297.6 54.6 %all-gather.8.cloned.1.call-done = bf16[512,4608]{1,0:T(8,128)(2,1)} async-done(((bf16[32,4608]{1,0:T(8,128)(2,1)}), bf16[512,4608]{1,0:T(8,128)(2,1)}) %all-gather.8.cloned.1.call-update) | async-done | bytes 4718608 | tf_op jit(solution)/shard_map/all_gather | solution.py:28
  352.2 7.4 %fusion.85 = f32[512,640]{1,0:T(8,128)S(1)} fusion(bf16[512,4608]{1,0:T(8,128)(2,1)} %all-gather.8.cloned.1.call-done, bf16[4608,640]{1,0:T(8,128)(2,1)} %param.28), kind=kOutput, calls=%fused_computation.141 | convolution fusion | flops 3019898880 | bytes 11927552 | tf_op jit(solution)/shard_map/dot_general | solution.py:221
  359.6 14.3 %convolution_convert_fusion = bf16[512,4608]{1,0:T(8,128)(2,1)} fusion(bf16[640,4608]{1,0:T(8,128)(2,1)} %param.30, bf16[512,4608]{1,0:T(8,128)(2,1)} %all-gather.8.cloned.1.call-done, bf16[4608,640]{1,0:T(8,128)(2,1)} %param.29, f32[512,640]{1,0:T(8,128)S(1)} %fusion.85), kind=kOutput, calls=%fused_computation.5 | convolution fusion | flops 6045433856 | bytes 22544384 | tf_op jit(solution)/shard_map/dot_general | solution.py:225
  374.0 78.9 %reduce-scatter.9.cloned.1.call-done = bf16[32,4608]{1,0:T(8,128)(2,1)} async-done(((bf16[512,4608]{1,0:T(8,128)(2,1)}), bf16[32,4608]{1,0:T(8,128)(2,1)}) %reduce-scatter.9.cloned.1.call-update) | async-done | bytes 294928 | tf_op jit(solution)/shard_map/reduce_scatter | solution.py:34
  453.8 15.4 %reduce-scatter.11.cloned.1.call-done = bf16[16,4608]{1,0:T(8,128)(2,1)} async-done(((bf16[32,4608]{1,0:T(8,128)(2,1)}), bf16[16,4608]{1,0:T(8,128)(2,1)}) %reduce-scatter.11.cloned.1.call-update) | async-done | bytes 147472 | tf_op jit(solution)/shard_map/reduce_scatter | solution.py:34
  (109 shorter events, 26.6 us)
Async XLA Ops:
  7.2 183.9 %copy-start = (bf16[128,4608]{1,0:T(8,128)(2,1)S(1)}, bf16[128,4608]{1,0:T(8,128)(2,1)}, u32[]{:S(2)}) copy-start(bf16[128,4608]{1,0:T(8,128)(2,1)} %param.27) | copy-start | bytes 3538948
  7.2 31.8 %all-gather.4.cloned.1.call-start = ((), (), s32[]{:S(2)}) async-start(), calls=%async_computation.4 | async-start | bytes 2621440 | tf_op jit(solution)/shard_map/all_gather | solution.py:184
  7.9 86.1 %all-gather.6.cloned.1.call-start = ((), (), s32[]{:S(2)}) async-start(), calls=%async_computation.5 | async-start | bytes 5013504 | tf_op jit(solution)/shard_map/all_gather | solution.py:28
  16.7 255.9 %reduce-scatter.5.cloned.1.call-start = ((), (), s32[]{:S(2)}) async-start(), calls=%async_computation.6 | async-start | bytes 5013504 | tf_op jit(solution)/shard_map/reduce_scatter | solution.py:34
  23.0 5.7 %copy-start.9 = (s32[1,512]{1,0:T(1,128)S(1)}, s32[1,512]{1,0:T(1,128)}, u32[]{:S(2)}) copy-start(s32[1,512]{1,0:T(1,128)} %param.36) | copy-start | bytes 6148
  23.0 5.7 %copy-start.18 = (s32[1,8]{1,0:T(1,128)S(1)}, s32[1,8]{1,0:T(1,128)}, u32[]{:S(2)}) copy-start(s32[1,8]{1,0:T(1,128)} %param.37) | copy-start | bytes 100
  23.0 5.8 %copy-start.19 = (s32[64]{0:T(128)S(1)}, s32[64]{0:T(128)}, u32[]{:S(2)}) copy-start(s32[64]{0:T(128)} %param.38) | copy-start | bytes 772
  27.5 116.8 %copy-start.3 = (bf16[256,4608]{1,0:T(8,128)(2,1)S(1)}, bf16[256,4608]{1,0:T(8,128)(2,1)}, u32[]{:S(2)}) copy-start(bf16[256,4608]{1,0:T(8,128)(2,1)} %copy.50) | copy-start | bytes 7077892
  143.0 5.3 %slice-start = ((s8[4718592]{0:T(1024)(128)(4,1)}), s8[4194304]{0:T(1024)(128)(4,1)S(1)}, s32[]{:S(2)}) async-start(s8[4718592]{0:T(1024)(128)(4,1)} %bitcast.100), calls=%async_computation.11 | async-start | bytes 8388608
  144.3 4.0 slice-start.1
  144.3 4.0 copy-start.5
  148.3 2.4 copy-start.8
  148.3 2.4 copy-start.10
  151.7 37.9 %copy-start.6 = (bf16[2,16,4608]{2,1,0:T(8,128)(2,1)S(1)}, bf16[2,16,4608]{2,1,0:T(8,128)(2,1)}, u32[]{:S(2)}) copy-start(bf16[2,16,4608]{2,1,0:T(8,128)(2,1)} %param.35) | copy-start | bytes 884740
  151.7 37.9 %copy-start.15 = (bf16[512,2]{0,1:T(2,128)(2,1)S(1)}, bf16[512,2]{0,1:T(2,128)(2,1)}, u32[]{:S(2)}) copy-start(bf16[512,2]{0,1:T(2,128)(2,1)} %get-tuple-element.14) | copy-start | bytes 6148
  194.6 95.3 %copy-start.4 = (bf16[16,4608]{1,0:T(8,128)(2,1)S(1)}, bf16[16,4608]{1,0:T(8,128)(2,1)}, u32[]{:S(2)}) copy-start(bf16[16,4608]{1,0:T(8,128)(2,1)} %param.20) | copy-start | bytes 442372
  194.6 95.3 %copy-start.11 = (f32[4608]{0:T(1024)S(1)}, f32[4608]{0:T(1024)}, u32[]{:S(2)}) copy-start(f32[4608]{0:T(1024)} %param.22) | copy-start | bytes 55300
  194.6 96.5 %copy-start.12 = (f32[4608]{0:T(1024)S(1)}, f32[4608]{0:T(1024)}, u32[]{:S(2)}) copy-start(f32[4608]{0:T(1024)} %param.23) | copy-start | bytes 55300
  194.6 94.2 %reduce-scatter.7.cloned.1.call-start = ((), (), s32[]{:S(2)}) async-start(), calls=%async_computation.7 | async-start | bytes 442368 | tf_op jit(solution)/shard_map/reduce_scatter | solution.py:34
  272.6 79.5 %all-gather.8.cloned.1.call-start = ((), (), s32[]{:S(2)}) async-start(), calls=%async_computation.8 | async-start | bytes 5013504 | tf_op jit(solution)/shard_map/all_gather | solution.py:28
  297.4 155.5 %reduce-scatter.9.cloned.1.call-start = ((), (), s32[]{:S(2)}) async-start(), calls=%async_computation.9 | async-start | bytes 5013504 | tf_op jit(solution)/shard_map/reduce_scatter | solution.py:34
  359.6 112.5 %copy-start.1 = (bf16[128,4608]{1,0:T(8,128)(2,1)S(1)}, bf16[128,4608]{1,0:T(8,128)(2,1)}, u32[]{:S(2)}) copy-start(bf16[128,4608]{1,0:T(8,128)(2,1)} %param.27) | copy-start | bytes 3538948
  373.9 96.5 %copy-start.13 = (f32[4608]{0:T(1024)S(1)}, f32[4608]{0:T(1024)}, u32[]{:S(2)}) copy-start(f32[4608]{0:T(1024)} %param.24) | copy-start | bytes 55300
  373.9 95.4 %reduce-scatter.11.cloned.1.call-start = ((), (), s32[]{:S(2)}) async-start(), calls=%async_computation.10 | async-start | bytes 442368 | tf_op jit(solution)/shard_map/reduce_scatter | solution.py:34
  (6 other events, 9.8 us)
Sparse Core Ops, SparseCore 0:
  9.7 29.2 all-gather.3
  41.1 52.8 all-gather.5
  194.7 77.8 reduce-scatter.4
  274.8 13.9 reduce-scatter.6
  297.5 54.6 all-gather.7
  374.1 78.8 reduce-scatter.8
  455.3 13.9 reduce-scatter.10

commit v3 on v2

--- a/solution.py
+++ b/solution.py
@@ -20,24 +20,38 @@
 
 DP_AXES = ("zh", "c")
 MP_AXES = ("x", "y", "zl")
-MP_STAGES = (("zl",), ("x", "y"))
+
+
+AXIS_SIZES = {"zh": 2, "c": 2, "x": 4, "y": 4, "zl": 2}
+PAIR_SWAP = ((0, 1), (1, 0))
 
 
 def gather_mp(values):
-    for stage in MP_STAGES:
-        values = lax.all_gather(values, stage, axis=0, tiled=True)
-    return values
+    other = lax.ppermute(values, "zl", perm=PAIR_SWAP)
+    lead = lax.axis_index("zl") == 0
+    values = jnp.concatenate(
+        [jnp.where(lead, values, other), jnp.where(lead, other, values)], axis=0
+    )
+    return lax.all_gather(values, ("x", "y"), axis=0, tiled=True)
 
 
 def scatter_mp(values):
-    for stage in reversed(MP_STAGES):
-        values = lax.psum_scatter(values, stage, scatter_dimension=0, tiled=True)
-    return values
+    values = lax.psum_scatter(values, ("x", "y"), scatter_dimension=0, tiled=True)
+    half = values.shape[0] // 2
+    lead = lax.axis_index("zl") == 0
+    keep = jnp.where(lead, values[:half], values[half:])
+    send = jnp.where(lead, values[half:], values[:half])
+    other = lax.ppermute(send, "zl", perm=PAIR_SWAP)
+    return keep.astype(jnp.float32) + other.astype(jnp.float32)
 
 
 def sum_mp(values):
-    for stage in (("zl",), ("y",), ("x",)):
-        values = lax.psum(values, stage)
+    for name in ("zl", "y", "x"):
+        step = 1
+        while step < AXIS_SIZES[name]:
+            partner = [(i, i ^ step) for i in range(AXIS_SIZES[name])]
+            values = values + lax.ppermute(values, name, perm=partner)
+            step *= 2
     return values
 
 

time: 480 us -> 409 us (0.85)
  blocking collectives: 93.7 us -> 0 us
  starting transfers between devices: 0.46 us -> 24.8 us
  other arithmetic: 13.3 us -> 20.8 us
    psum x6 -> x0, blocking collectives: 80.9 us -> none  [sum_mp(): values = lax.psum(values, stage)]
    ppermute x0 -> x14, waiting for transfers between devices: none -> 34.2 us  [the longest x10 20.5 us: sum_mp(): values = values + lax.ppermute(values, name, perm=partner)]
    reduce_scatter x4 -> x2, waiting for transfers between devices: 188 us -> 156 us  [scatter_mp(): lax.psum_scatter(values, ('x', 'y'), scatter_dimension=0, tiled=True)]
    ppermute x0 -> x14, starting transfers between devices: none -> 24.6 us  [the longest x10 17.6 us: sum_mp(): values = values + lax.ppermute(values, name, perm=partner)]
    all_gather x2 -> x0, blocking collectives: 12.8 us -> none  [gather_mp(): values = lax.all_gather(values, stage, axis=0, tiled=True)]
  transfers between devices with their start and end apart: 7 -> 19, of which waited for: 7 -> 17; matrix products, arithmetic and copies ran while one was open for 5% -> 7% of each run, Pallas kernels for 0% -> 0%
where the time goes in v3:
time: 409 us
  waiting for transfers between devices  298 us (73%)
  matrix products  38.7 us (9%)
  starting transfers between devices  24.8 us (6%)
  other arithmetic  20.8 us (5%)
  between operations  14.2 us (3%)
  local copies, waits for them, and re-layouts  12.3 us (3%)
    reduce_scatter x2, waiting for transfers between devices, scatter_mp(): lax.psum_scatter(values, ('x', 'y'), scatter_dimension=0, tiled=True)  156 us
    all_gather x2, waiting for transfers between devices, gather_mp(): return lax.all_gather(values, ('x', 'y'), axis=0, tiled=True)  103 us
    ppermute x10, waiting for transfers between devices, sum_mp(): values = values + lax.ppermute(values, name, perm=partner)  20.5 us
    ppermute x10, starting transfers between devices, sum_mp(): values = values + lax.ppermute(values, name, perm=partner)  17.6 us
    dot_general x1, matrix products, shards(): jnp.dot(hidden, down_matrix, preferred_element_type=jnp.float32)  14.3 us
  transfers between devices with their start and end apart: 19, of which 17 were waited for; matrix products, arithmetic and copies ran while one was open for 7% of the time, Pallas kernels for 0%

profile of v3, /device:TPU:0, one launch (start us, length us, event | category | flops | bytes accessed | tf_op | source)
XLA Modules:
  0.0 408.6 jit_solution(608620565945825807)
XLA Ops:
  11.6 3.8 collective-permute-done
  23.4 49.8 %all-gather.6.cloned.1.call-done = bf16[512,4608]{1,0:T(8,128)(2,1)} async-done(((bf16[32,4608]{1,0:T(8,128)(2,1)}), bf16[512,4608]{1,0:T(8,128)(2,1)}) %all-gather.6.cloned.1.call-update) | async-done | bytes 4718608 | tf_op jit(solution)/shard_map/all_gather | solution.py:35
  73.3 3.9 fusion.79
  85.7 3.0 collective-permute-start.3
  94.8 2.5 copy.52
  97.3 4.1 %all-gather.4.cloned.1.call-done = bf16[256,2,1,16,128]{4,3,2,1,0:T(8,128)(2,1)} async-done(((bf16[64,2,1,16,128]{4,3,2,1,0:T(8,128)(2,1)}), bf16[256,2,1,16,128]{4,3,2,1,0:T(8,128)(2,1)}) %all-gather.4.cloned.1.call-update) | async-done | bytes 2097168 | tf_op jit(solution)/shard_map/all_gather | solution.py:198
  101.4 2.3 gather_fusion
  106.0 2.4 collective-permute-done.4
  108.5 3.0 collective-permute-start.5
  111.5 4.6 %fusion.19 = f32[512,2,1,128]{0,3,2,1:T(8,128)S(1)} fusion(bf16[2,128,4608]{2,1,0:T(8,128)(2,1)} %bitcast.105, bf16[512,4608]{1,0:T(8,128)(2,1)} %all-gather.6.cloned.1.call-done), kind=kOutput, calls=%fused_computation.30 | convolution fusion | flops 1207959552 | bytes 7602176 | tf_op jit(solution)/shard_map/dot_general | solution.py:153
  121.3 3.3 collective-permute-done.6
  126.1 2.4 collective-permute-done.7
  128.5 3.3 collective-permute-start.8
  134.5 3.3 collective-permute-done.9
  140.3 3.2 collective-permute-done.10
  143.6 3.5 fusion
  147.2 76.9 %reduce-scatter.3.cloned.1.call-done = bf16[32,4608]{1,0:T(8,128)(2,1)} async-done(((bf16[512,4608]{1,0:T(8,128)(2,1)}), bf16[32,4608]{1,0:T(8,128)(2,1)}) %reduce-scatter.3.cloned.1.call-update) | async-done | bytes 294928 | tf_op jit(solution)/shard_map/reduce_scatter | solution.py:39
  226.8 3.6 collective-permute-done.11
  234.5 3.6 collective-permute-done.12
  239.1 53.0 %all-gather.8.cloned.1.call-done = bf16[512,4608]{1,0:T(8,128)(2,1)} async-done(((bf16[32,4608]{1,0:T(8,128)(2,1)}), bf16[512,4608]{1,0:T(8,128)(2,1)}) %all-gather.8.cloned.1.call-update) | async-done | bytes 4718608 | tf_op jit(solution)/shard_map/all_gather | solution.py:35
  292.1 7.4 %fusion.81 = f32[512,640]{1,0:T(8,128)S(1)} fusion(bf16[512,4608]{1,0:T(8,128)(2,1)} %all-gather.8.cloned.1.call-done, bf16[4608,640]{1,0:T(8,128)(2,1)} %param.28), kind=kOutput, calls=%fused_computation.149 | convolution fusion | flops 3019898880 | bytes 11927552 | tf_op jit(solution)/shard_map/dot_general | solution.py:235
  299.6 14.3 %convolution_convert_fusion = bf16[512,4608]{1,0:T(8,128)(2,1)} fusion(bf16[640,4608]{1,0:T(8,128)(2,1)} %param.30, bf16[512,4608]{1,0:T(8,128)(2,1)} %all-gather.8.cloned.1.call-done, bf16[4608,640]{1,0:T(8,128)(2,1)} %param.29, f32[512,640]{1,0:T(8,128)S(1)} %fusion.81), kind=kOutput, calls=%fused_computation.5 | convolution fusion | flops 6045433856 | bytes 22544384 | tf_op jit(solution)/shard_map/dot_general | solution.py:239
  313.9 79.0 %reduce-scatter.5.cloned.1.call-done = bf16[32,4608]{1,0:T(8,128)(2,1)} async-done(((bf16[512,4608]{1,0:T(8,128)(2,1)}), bf16[32,4608]{1,0:T(8,128)(2,1)}) %reduce-scatter.5.cloned.1.call-update) | async-done | bytes 294928 | tf_op jit(solution)/shard_map/reduce_scatter | solution.py:39
  396.4 2.7 collective-permute-done.13
  (127 shorter events, 55.2 us)
Async XLA Ops:
  7.2 131.8 %copy-start = (bf16[128,4608]{1,0:T(8,128)(2,1)S(1)}, bf16[128,4608]{1,0:T(8,128)(2,1)}, u32[]{:S(2)}) copy-start(bf16[128,4608]{1,0:T(8,128)(2,1)} %param.27) | copy-start | bytes 3538948
  7.2 66.1 %all-gather.6.cloned.1.call-start = ((), (), s32[]{:S(2)}) async-start(), calls=%async_computation.3 | async-start | bytes 5013504 | tf_op jit(solution)/shard_map/all_gather | solution.py:35
  9.4 6.0 %collective-permute-start = (bf16[16,4608]{1,0:T(8,128)(2,1)S(1)}, bf16[16,4608]{1,0:T(8,128)(2,1)S(1)}, u32[]{:S(2)}, u32[]{:S(2)}) collective-permute-start(bf16[16,4608]{1,0:T(8,128)(2,1)S(1)} %fusion.29), channel_id=1, source_target_pairs={{0,1},{1,0},{2,3},{3,2},{4,5},{5,4},{6,7},{7,6},{8,9},{9,8},{10,11... | collective-permute-start | bytes 442376 | tf_op jit(solution)/shard_map/ppermute | solution.py:30
  17.3 84.2 %all-gather.4.cloned.1.call-start = ((), (), s32[]{:S(2)}) async-start(), calls=%async_computation.2 | async-start | bytes 2621440 | tf_op jit(solution)/shard_map/all_gather | solution.py:198
  18.0 206.1 %reduce-scatter.3.cloned.1.call-start = ((), (), s32[]{:S(2)}) async-start(), calls=%async_computation.4 | async-start | bytes 5013504 | tf_op jit(solution)/shard_map/reduce_scatter | solution.py:39
  77.1 4.0 collective-permute-start.1
  81.1 3.9 collective-permute-start.2
  85.7 18.1 %collective-permute-start.3 = (f32[512,16]{0,1:T(8,128)}, f32[512,16]{0,1:T(8,128)}, u32[]{:S(2)}, u32[]{:S(2)}) collective-permute-start(f32[512,16]{0,1:T(8,128)} %add.209), channel_id=1, source_target_pairs={{0,4},{2,6},{4,0},{6,2},{1,5},{3,7},{5,1},{7,3},{8,12},{10,14},{12... | collective-permute-start | bytes 98312 | tf_op jit(solution)/shard_map/ppermute | solution.py:53
  104.6 3.9 collective-permute-start.4
  108.5 7.6 %collective-permute-start.5 = (f32[512,16]{0,1:T(8,128)S(1)}, f32[512,16]{0,1:T(8,128)S(1)}, u32[]{:S(2)}, u32[]{:S(2)}) collective-permute-start(f32[512,16]{0,1:T(8,128)S(1)} %add.211), channel_id=1, source_target_pairs={{0,16},{8,24},{16,0},{24,8},{1,17},{9,25},{17,1},{25,9},{2,18},{10... | collective-permute-start | bytes 98312 | tf_op jit(solution)/shard_map/ppermute | solution.py:53
  120.6 4.0 collective-permute-start.6
  124.6 3.9 collective-permute-start.7
  128.5 5.4 %collective-permute-start.8 = (f32[512,16]{0,1:T(8,128)S(1)}, f32[512,16]{0,1:T(8,128)S(1)}, u32[]{:S(2)}, u32[]{:S(2)}) collective-permute-start(f32[512,16]{0,1:T(8,128)S(1)} %add.225), channel_id=1, source_target_pairs={{0,4},{2,6},{4,0},{6,2},{1,5},{3,7},{5,1},{7,3},{8,12},{10,14},{12... | collective-permute-start | bytes 98312 | tf_op jit(solution)/shard_map/ppermute | solution.py:53
  134.0 3.9 collective-permute-start.9
  137.9 5.7 %collective-permute-start.10 = (f32[512,16]{0,1:T(8,128)S(1)}, f32[512,16]{0,1:T(8,128)S(1)}, u32[]{:S(2)}, u32[]{:S(2)}) collective-permute-start(f32[512,16]{0,1:T(8,128)S(1)} %add.227), channel_id=1, source_target_pairs={{0,16},{8,24},{16,0},{24,8},{1,17},{9,25},{17,1},{25,9},{2,18},{10... | collective-permute-start | bytes 98312 | tf_op jit(solution)/shard_map/ppermute | solution.py:53
  147.1 84.4 %copy-start.11 = (f32[4608]{0:T(1024)S(1)}, f32[4608]{0:T(1024)}, u32[]{:S(2)}) copy-start(f32[4608]{0:T(1024)} %param.22) | copy-start | bytes 55300
  147.1 85.7 %copy-start.8 = (f32[4608]{0:T(1024)S(1)}, f32[4608]{0:T(1024)}, u32[]{:S(2)}) copy-start(f32[4608]{0:T(1024)} %param.23) | copy-start | bytes 55300
  147.2 145.0 %all-gather.8.cloned.1.call-start = ((), (), s32[]{:S(2)}) async-start(), calls=%async_computation.5 | async-start | bytes 5013504 | tf_op jit(solution)/shard_map/all_gather | solution.py:35
  225.1 5.2 %collective-permute-start.11 = (bf16[16,4608]{1,0:T(8,128)(2,1)S(1)}, bf16[16,4608]{1,0:T(8,128)(2,1)S(1)}, u32[]{:S(2)}, u32[]{:S(2)}) collective-permute-start(bf16[16,4608]{1,0:T(8,128)(2,1)S(1)} %broadcast_select_fusion.4), channel_id=1, source_target_pairs={{0,1},{1,0},{2,3},{3,2},{4,5},{5,4},{6,7},{7,6},{8,9},{9,8},{10,11... | collective-permute-start | bytes 442376 | tf_op jit(solution)/shard_map/ppermute | solution.py:44
  232.9 5.2 %collective-permute-start.12 = (bf16[16,4608]{1,0:T(8,128)(2,1)S(1)}, bf16[16,4608]{1,0:T(8,128)(2,1)S(1)}, u32[]{:S(2)}, u32[]{:S(2)}) collective-permute-start(bf16[16,4608]{1,0:T(8,128)(2,1)S(1)} %fusion.33), channel_id=1, source_target_pairs={{0,1},{1,0},{2,3},{3,2},{4,5},{5,4},{6,7},{7,6},{8,9},{9,8},{10,11... | collective-permute-start | bytes 442376 | tf_op jit(solution)/shard_map/ppermute | solution.py:30
  239.0 153.9 %reduce-scatter.5.cloned.1.call-start = ((), (), s32[]{:S(2)}) async-start(), calls=%async_computation.6 | async-start | bytes 5013504 | tf_op jit(solution)/shard_map/reduce_scatter | solution.py:39
  299.5 102.5 %copy-start.1 = (bf16[128,4608]{1,0:T(8,128)(2,1)S(1)}, bf16[128,4608]{1,0:T(8,128)(2,1)}, u32[]{:S(2)}) copy-start(bf16[128,4608]{1,0:T(8,128)(2,1)} %param.27) | copy-start | bytes 3538948
  313.9 86.4 %copy-start.10 = (f32[4608]{0:T(1024)S(1)}, f32[4608]{0:T(1024)}, u32[]{:S(2)}) copy-start(f32[4608]{0:T(1024)} %param.24) | copy-start | bytes 55300
  393.9 5.2 %collective-permute-start.13 = (bf16[16,4608]{1,0:T(8,128)(2,1)S(1)}, bf16[16,4608]{1,0:T(8,128)(2,1)S(1)}, u32[]{:S(2)}, u32[]{:S(2)}) collective-permute-start(bf16[16,4608]{1,0:T(8,128)(2,1)S(1)} %broadcast_select_fusion), channel_id=1, source_target_pairs={{0,1},{1,0},{2,3},{3,2},{4,5},{5,4},{6,7},{7,6},{8,9},{9,8},{10,11... | collective-permute-start | bytes 442376 | tf_op jit(solution)/shard_map/ppermute | solution.py:44
  (12 other events, 206.5 us)
Sparse Core Ops, SparseCore 0:
  17.4 55.8 all-gather.5
  74.9 26.4 all-gather.3
  147.3 76.8 reduce-scatter.2
  239.2 52.9 all-gather.7
  314.0 78.8 reduce-scatter.4
